TPU v7x, 512 devices: a whole 4x4x16 slice. The times are simulated.
512 devices in a mesh: dp: 16 (over z), row: 4 (over y), col: 8 (over x, core).
Axes of the slice: x: 4, y: 4, z: 16, core: 2. Of those that a mesh axis runs over, the one named last changes fastest.
Arguments:
- layer_input: bfloat16 [3072, 4096], P(('dp', 'col'), 'row'), may hold values from -6 to 6
- hidden_grad: bfloat16 [3072, 14336], P(('dp', 'row'), 'col'), may hold values from -6 to 6
- gate_slots: bfloat16 [4, 8, 48, 128, 128], P('row', 'col', 'dp'), may hold values from -0.125 to 0.125
- up_slots: bfloat16 [4, 8, 48, 128, 128], P('row', 'col', 'dp'), may hold values from -0.125 to 0.125
- block_mask: int32 [32, 112], replicated, may hold values from 0 to 1, as said below
Outputs:
- input_grad: bfloat16 [3072, 4096], P(('dp', 'col'), 'row')
- gate_slot_grad: float32 [4, 8, 48, 128, 128], P('row', 'col', 'dp')
- up_slot_grad: float32 [4, 8, 48, 128, 128], P('row', 'col', 'dp')
Inputs may be any that keep to these rules, and one draw needn't show every extreme that they name: `block_mask`: every tile of 8 x 14 blocks keeps between 24 and 48 blocks; some tile keeps exactly 48, which tile depends on the draw.
All inputs are finite; a program needn't handle non-finite values.
Results may differ from a plain program's by a relative error of at most 0.022.
Values may be sent and summed in bfloat16 or wider, within the bound.
No kernel may reach another device: no remote copies, remote signals or barrier semaphores. Data moves between devices by JAX's collectives and lax.ppermute only.
A program may use at most 64 MiB of HBM per device.

v0:
```python
import jax
import jax.numpy as jnp
from jax import lax
from jax.sharding import PartitionSpec as P


def slot_maps(block_mask, tile_rows, tile_cols, capacity):
    row_first = lax.axis_index("row") * tile_rows
    col_first = lax.axis_index("col") * tile_cols
    tile_mask = lax.dynamic_slice(block_mask, (row_first, col_first), (tile_rows, tile_cols))
    flat_mask = tile_mask.reshape(tile_rows * tile_cols)
    position = jnp.cumsum(flat_mask) - 1
    slot_ids = jnp.arange(capacity, dtype=jnp.int32)
    chosen = ((flat_mask[:, None] > 0) & (position[:, None] == slot_ids[None, :])).astype(jnp.int32)
    block_ids = jnp.arange(tile_rows * tile_cols, dtype=jnp.int32)
    slot_block = jnp.sum(chosen * block_ids[:, None], axis=0)
    live_slots = jnp.sum(chosen, axis=0).astype(jnp.float32)
    slot_row = slot_block // tile_cols
    slot_col = slot_block % tile_cols
    col_table = (slot_col[:, None] == jnp.arange(tile_cols, dtype=jnp.int32)[None, :]).astype(
        jnp.float32
    ) * live_slots[:, None]
    row_table = (slot_row[:, None] == jnp.arange(tile_rows, dtype=jnp.int32)[None, :]).astype(
        jnp.float32
    ) * live_slots[:, None]
    return (slot_row, slot_col, live_slots, col_table, row_table)


def slot_products(picked, pair_weights, col_table):
    per_slot = jnp.einsum("tsk,skn->tsn", picked, pair_weights, preferred_element_type=jnp.float32)
    return jnp.einsum("tsn,sc->tcn", per_slot, col_table, precision=lax.Precision.HIGHEST)


def back_products(grad_picked, pair_weights, row_table):
    per_slot = jnp.einsum(
        "tsn,skn->tsk", grad_picked, pair_weights, preferred_element_type=jnp.float32
    )
    return jnp.einsum("tsk,sr->trk", per_slot, row_table, precision=lax.Precision.HIGHEST)


def on_device(layer_input, hidden_grad, gate_slots, up_slots, block_mask):
    gate_local = gate_slots[0, 0]
    up_local = up_slots[0, 0]
    block_size = gate_local.shape[-1]
    replicas = lax.axis_size("dp")
    capacity = gate_local.shape[0] * replicas
    token_panel = lax.all_gather(layer_input, "col", axis=0, tiled=True)
    grad_panel = lax.all_gather(hidden_grad, "row", axis=0, tiled=True)
    tok_rows = token_panel.shape[0]
    feat_cols = token_panel.shape[1]
    unit_cols = grad_panel.shape[1]
    tile_rows = feat_cols // block_size
    tile_cols = unit_cols // block_size
    slot_row, slot_col, live_slots, col_table, row_table = slot_maps(
        block_mask, tile_rows, tile_cols, capacity
    )
    token_blocks = token_panel.reshape(tok_rows, tile_rows, block_size)
    picked_tokens = jnp.take(token_blocks, slot_row, axis=1)
    gate_all, up_all = (
        lax.all_gather(gate_local, "dp", axis=0, tiled=True),
        lax.all_gather(up_local, "dp", axis=0, tiled=True),
    )
    pair_all = jnp.concatenate([gate_all, up_all], axis=2)
    pair_part = slot_products(picked_tokens, pair_all, col_table)
    gate_part = pair_part[:, :, :block_size].reshape(tok_rows, unit_cols)
    up_part = pair_part[:, :, block_size:].reshape(tok_rows, unit_cols)
    gate_sum, up_sum = (
        lax.psum(gate_part.astype(jnp.bfloat16), "row").astype(jnp.float32),
        lax.psum(up_part.astype(jnp.bfloat16), "row").astype(jnp.float32),
    )
    sigmoid_gate = jax.nn.sigmoid(gate_sum)
    upstream = grad_panel.astype(jnp.float32)
    gate_grad = (upstream * up_sum * sigmoid_gate * (1.0 + gate_sum * (1.0 - sigmoid_gate))).astype(
        jnp.bfloat16
    )
    up_grad = (upstream * gate_sum * sigmoid_gate).astype(jnp.bfloat16)
    grad_pair = jnp.concatenate(
        [
            gate_grad.reshape(tok_rows, tile_cols, block_size),
            up_grad.reshape(tok_rows, tile_cols, block_size),
        ],
        axis=2,
    )
    grad_picked = jnp.take(grad_pair, slot_col, axis=1)
    summed = back_products(grad_picked, pair_all, row_table)
    input_sum = lax.psum_scatter(
        summed.reshape(tok_rows // lax.axis_size("col") * lax.axis_size("col"), feat_cols).astype(
            jnp.bfloat16
        ),
        "col",
        scatter_dimension=0,
        tiled=True,
    )
    pair_term = (
        jnp.einsum("tsk,tsn->skn", picked_tokens, grad_picked, preferred_element_type=jnp.float32)
        * live_slots[:, None, None]
    )
    pair_total = lax.psum_scatter(
        pair_term.astype(jnp.bfloat16), "dp", scatter_dimension=0, tiled=True
    ).astype(jnp.float32)
    gate_out = (pair_total[:, :, :block_size] / replicas)[None, None]
    up_out = (pair_total[:, :, block_size:] / replicas)[None, None]
    return (input_sum, gate_out, up_out)


def solution(mesh):
    return jax.shard_map(
        on_device,
        mesh=mesh,
        in_specs=(
            P(("dp", "col"), "row"),
            P(("dp", "row"), "col"),
            P("row", "col", "dp", None, None),
            P("row", "col", "dp", None, None),
            P(),
        ),
        out_specs=(
            P(("dp", "col"), "row"),
            P("row", "col", "dp", None, None),
            P("row", "col", "dp", None, None),
        ),
        check_vma=False,
    )
```

profile of v0, /device:TPU:8, one launch (start us, length us, event | category | flops | bytes accessed | tf_op | source)
XLA Modules:
  0.0 370.0 jit_solution(6575437389521833175)
XLA Ops:
  7.2 0.7 all-gather.5.cloned.1.call-update
  7.9 0.7 all-gather.7.cloned.1.call-update
  8.7 0.8 broadcast_compare_fusion
  10.1 13.5 %all_gather.15 = bf16[192,1024]{1,0:T(8,128)(2,1)S(1)} all-gather(bf16[24,1024]{1,0:T(8,128)(2,1)} %param.5), channel_id=1, replica_groups=mesh['dp'=16,'row'=4,'col'=8] {'col'}, dimensions={0}, use_global_device_ids=true | all-gather | bytes 442368 | tf_op jit(solution)/shard_map/all_gather | solution.py:47
  23.7 1.0 gather_fusion
  24.7 61.7 %all-gather.5.cloned.1.call-done = bf16[1,1,48,128,128]{4,3,1,0,2:T(8,128)(2,1)} async-done(((bf16[1,1,3,128,128]{4,3,1,0,2:T(8,128)(2,1)}), bf16[1,1,48,128,128]{4,3,1,0,2:T(8,128)(2,1)}) %all-gather.5.cloned.1.call-update) | async-done | bytes 1572880 | tf_op jit(solution)/shard_map/all_gather | solution.py:60
  86.4 71.1 %all-gather.7.cloned.1.call-done = bf16[1,1,48,128,128]{4,3,1,0,2:T(8,128)(2,1)} async-done(((bf16[1,1,3,128,128]{4,3,1,0,2:T(8,128)(2,1)}), bf16[1,1,48,128,128]{4,3,1,0,2:T(8,128)(2,1)}) %all-gather.7.cloned.1.call-update) | async-done | bytes 1572880 | tf_op jit(solution)/shard_map/all_gather | solution.py:61
  157.5 3.3 convolution_bitcast_fusion
  160.8 9.9 %fusion.20 = bf16[192,14,256]{2,1,0:T(8,128)(2,1)S(1)} fusion(f32[192,48,256]{2,0,1:T(8,128)S(1)} %convolution_bitcast_fusion, f32[48]{0:T(128)S(1)} %convert_element_type.55, s32[48]{0:T(128)S(1)} %get-tuple-element.8), kind=kOutput, calls=%fused_computation.23 | convolution fusion | flops 397051200 | bytes 10813824 | tf_op jit(solution)/shard_map/tsn,sc->tcn/dot_general | solution.py:31
  171.0 1.0 copy.56
  172.1 1.1 copy.57
  173.2 13.2 %all_gather.14 = bf16[192,1792]{1,0:T(8,128)(2,1)S(1)} all-gather(bf16[48,1792]{1,0:T(8,128)(2,1)S(1)} %copy-done.3), channel_id=1, replica_groups=mesh['dp'=16,'row'=4,'col'=8] {'row'}, dimensions={0}, use_global_device_ids=true | all-gather | bytes 860160 | tf_op jit(solution)/shard_map/all_gather | solution.py:48
  186.4 46.7 %all-reduce.3.cloned.1.call-done = (bf16[192,1792]{1,0:T(8,128)(2,1)}, bf16[192,1792]{1,0:T(8,128)(2,1)}) async-done(((bf16[192,1792]{1,0:T(8,128)(2,1)}, bf16[192,1792]{1,0:T(8,128)(2,1)}), (bf16[192,1792]{1,0:T(8,128)(2,1)}, bf16[192,1792]{1,0:T(8,128)(2,1)})) %all-reduce.3.cloned.1.call-update) | async-done | bytes 1376272 | tf_op jit(solution)/shard_map/psum | solution.py:68
  233.1 2.1 fusion.36
  235.7 3.1 gather_fusion.1
  238.8 6.2 %multiply_convert_fusion = bf16[48,128,256]{2,1,0:T(8,128)(2,1)} fusion(f32[48]{0:T(128)S(1)} %convert_element_type.55, bf16[48,192,256]{2,1,0:T(8,128)(2,1)} %gather_fusion.1, pred[48]{0:T(512)(128)(4,1)S(1)} %get-tuple-element.7, bf16[48,192,128]{2,1,0:T(8,128)(2,1)} %copy-done, pred[48]{0:T(512)(128)(4,1)S(1)} %get-tuple-element.22), kind=kOutput, calls=%fused_computation.4 | convolution fusion | flops 610664448 | bytes 10223904 | tf_op jit(solution)/shard_map/tsk,tsn->skn/dot_general | solution.py:95
  245.1 1.3 copy-done.1
  246.9 3.3 fusion.10
  250.3 4.9 %fusion.32 = bf16[8,192,128]{2,0,1:T(8,128)(2,1)S(1)} fusion(f32[192,48,128]{2,0,1:T(8,128)S(1)} %fusion.10, f32[48]{0:T(128)S(1)} %convert_element_type.55, s32[48]{0:T(128)S(1)} %get-tuple-element.23), kind=kOutput, calls=%fused_computation.34 | convolution fusion | flops 113443584 | bytes 5112192 | tf_op jit(solution)/shard_map/tsk,sr->trk/dot_general | solution.py:38
  255.2 0.8 copy.60
  256.0 67.8 %reduce-scatter.5.cloned.1.call-done = bf16[3,128,256]{2,1,0:T(8,128)(2,1)} async-done(((bf16[48,128,256]{2,1,0:T(8,128)(2,1)}), bf16[3,128,256]{2,1,0:T(8,128)(2,1)}) %reduce-scatter.5.cloned.1.call-update) | async-done | bytes 196624 | tf_op jit(solution)/shard_map/reduce_scatter | solution.py:98
  323.8 1.0 convert_element_type.67
  324.8 0.8 fusion.37
  325.5 38.0 %reduce-scatter.3.cloned.1.call-done = bf16[24,1024]{1,0:T(8,128)(2,1)} async-done(((bf16[192,1024]{1,0:T(8,128)(2,1)}), bf16[24,1024]{1,0:T(8,128)(2,1)}) %reduce-scatter.3.cloned.1.call-update) | async-done | bytes 49168 | tf_op jit(solution)/shard_map/reduce_scatter | solution.py:86
  (29 shorter events, 2.2 us)
Async XLA Ops:
  7.2 79.3 %all-gather.5.cloned.1.call-start = ((), (), s32[]{:S(2)}) async-start(), calls=%async_computation.4 | async-start | bytes 1671168 | tf_op jit(solution)/shard_map/all_gather | solution.py:60
  7.9 149.6 %all-gather.7.cloned.1.call-start = ((), (), s32[]{:S(2)}) async-start(), calls=%async_computation.5 | async-start | bytes 1671168 | tf_op jit(solution)/shard_map/all_gather | solution.py:61
  8.6 224.4 %all-reduce.3.cloned.1.call-start = ((), (), s32[]{:S(2)}) async-start(), calls=%async_computation.6 | async-start | bytes 2752512 | tf_op jit(solution)/shard_map/psum | solution.py:68
  24.7 136.1 %copy-start = (bf16[48,192,128]{2,1,0:T(8,128)(2,1)}, bf16[48,192,128]{2,1,0:T(8,128)(2,1)S(1)}, u32[]{:S(2)}) copy-start(bf16[48,192,128]{2,1,0:T(8,128)(2,1)S(1)} %gather_fusion) | copy-start | bytes 7077892
  171.0 2.2 copy-start.3
  173.2 150.6 %reduce-scatter.5.cloned.1.call-start = ((), (), s32[]{:S(2)}) async-start(), calls=%async_computation.3 | async-start | bytes 3342336 | tf_op jit(solution)/shard_map/reduce_scatter | solution.py:98
  245.1 1.4 copy-start.1
  245.1 1.9 copy-start.2
  245.1 118.4 %reduce-scatter.3.cloned.1.call-start = ((), (), s32[]{:S(2)}) async-start(), calls=%async_computation.2 | async-start | bytes 442368 | tf_op jit(solution)/shard_map/reduce_scatter | solution.py:86
Sparse Core Ops, SparseCore 0:
  10.0 76.3 all-gather.4
  88.5 68.9 all-gather.6
  173.3 59.7 all-reduce.2
  245.2 78.5 reduce-scatter.4
  327.0 36.4 reduce-scatter.2
where the time goes:
time: 370 us
  waiting for transfers between devices  287 us (78%)
  matrix products  27.7 us (7%)
  blocking collectives  26.7 us (7%)
  between operations  13.9 us (4%)
  local copies, waits for them, and re-layouts  9.72 us (3%)
  other arithmetic  5.19 us (1%)
    all_gather x1, waiting for transfers between devices, on_device(): lax.all_gather(up_local, 'dp', axis=0, tiled=True)  71.1 us
    reduce_scatter x1, waiting for transfers between devices, on_device(): lax.psum_scatter(pair_term.astype(jnp.bfloat16), 'dp', scatter_dimension=...  67.8 us
    all_gather x1, waiting for transfers between devices, on_device(): lax.all_gather(gate_local, 'dp', axis=0, tiled=True)  61.7 us
    psum x1, waiting for transfers between devices, on_device(): lax.psum(gate_part.astype(jnp.bfloat16), 'row').astype(jnp.float32)  46.7 us
    reduce_scatter x1, waiting for transfers between devices, on_device(): lax.psum_scatter(summed.reshape(tok_rows // lax.axis_size('col') * lax.ax...  38 us
    all_gather x1, blocking collectives, on_device(): token_panel = lax.all_gather(layer_input, 'col', axis=0, tiled=True)  13.5 us
    all_gather x1, blocking collectives, on_device(): grad_panel = lax.all_gather(hidden_grad, 'row', axis=0, tiled=True)  13.2 us
    dot_general x1, matrix products, slot_products(): jnp.einsum('tsn,sc->tcn', per_slot, col_table, precision=lax.Precision.HI...  9.9 us
  transfers between devices with their start and end apart: 5, of which 5 were waited for; matrix products, arithmetic and copies ran while one was open for 4% of the time, Pallas kernels for 0%

commit v1 on v0

--- a/solution.py
+++ b/solution.py
@@ -65,7 +65,7 @@
     gate_part = pair_part[:, :, :block_size].reshape(tok_rows, unit_cols)
     up_part = pair_part[:, :, block_size:].reshape(tok_rows, unit_cols)
     gate_sum, up_sum = (
-        lax.psum(gate_part.astype(jnp.bfloat16), "row").astype(jnp.float32),
+        jnp.sum(lax.all_gather(gate_part.astype(jnp.bfloat16), "row"), axis=0).astype(jnp.float32),
         lax.psum(up_part.astype(jnp.bfloat16), "row").astype(jnp.float32),
     )
     sigmoid_gate = jax.nn.sigmoid(gate_sum)

time: 370 us -> 412 us (1.11)
  waiting for transfers between devices: 287 us -> 325 us
    all_gather x0 -> x1, waiting for transfers between devices: none -> 25.9 us  [on_device(): lax.all_gather(gate_part.astype(jnp.bfloat16), 'row')]
    psum x1, waiting for transfers between devices: 46.7 us -> 59.4 us  [on_device(): lax.psum(up_part.astype(jnp.bfloat16), 'row').astype(jnp.float32)]
  transfers between devices with their start and end apart: 5 -> 6, of which waited for: 5 -> 6; matrix products, arithmetic and copies ran while one was open for 4% -> 4% of each run, Pallas kernels for 0% -> 0%
where the time goes in v1:
time: 412 us; the launch traced here: 411 us
  waiting for transfers between devices  325 us (79%)
  matrix products  27.7 us (7%)
  blocking collectives  26.7 us (6%)
  between operations  14.3 us (3%)
  local copies, waits for them, and re-layouts  9.78 us (2%)
  other arithmetic  7.46 us (2%)
    all_gather x1, waiting for transfers between devices, on_device(): lax.all_gather(up_local, 'dp', axis=0, tiled=True)  71.1 us
    reduce_scatter x1, waiting for transfers between devices, on_device(): lax.psum_scatter(pair_term.astype(jnp.bfloat16), 'dp', scatter_dimension=...  67.6 us
    all_gather x1, waiting for transfers between devices, on_device(): lax.all_gather(gate_local, 'dp', axis=0, tiled=True)  61.7 us
    psum x1, waiting for transfers between devices, on_device(): lax.psum(up_part.astype(jnp.bfloat16), 'row').astype(jnp.float32)  59.4 us
    reduce_scatter x1, waiting for transfers between devices, on_device(): lax.psum_scatter(summed.reshape(tok_rows // lax.axis_size('col') * lax.ax...  37.9 us
    all_gather x1, waiting for transfers between devices, on_device(): lax.all_gather(gate_part.astype(jnp.bfloat16), 'row')  25.9 us
    all_gather x1, blocking collectives, on_device(): token_panel = lax.all_gather(layer_input, 'col', axis=0, tiled=True)  13.5 us
    all_gather x1, blocking collectives, on_device(): grad_panel = lax.all_gather(hidden_grad, 'row', axis=0, tiled=True)  13.2 us
  transfers between devices with their start and end apart: 6, of which 6 were waited for; matrix products, arithmetic and copies ran while one was open for 4% of the time, Pallas kernels for 0%

profile of v1, /device:TPU:8, one launch (start us, length us, event | category | flops | bytes accessed | tf_op | source)
XLA Modules:
  0.0 411.3 jit_solution(2873651495763141324)
XLA Ops:
  8.7 0.8 broadcast_compare_fusion
  10.1 13.5 %all_gather.19 = bf16[192,1024]{1,0:T(8,128)(2,1)S(1)} all-gather(bf16[24,1024]{1,0:T(8,128)(2,1)} %param.5), channel_id=1, replica_groups=mesh['dp'=16,'row'=4,'col'=8] {'col'}, dimensions={0}, use_global_device_ids=true | all-gather | bytes 442368 | tf_op jit(solution)/shard_map/all_gather | solution.py:47
  23.7 1.0 gather_fusion
  24.7 61.7 %all-gather.8.cloned.1.call-done = bf16[1,1,48,128,128]{4,3,1,0,2:T(8,128)(2,1)} async-done(((bf16[1,1,3,128,128]{4,3,1,0,2:T(8,128)(2,1)}), bf16[1,1,48,128,128]{4,3,1,0,2:T(8,128)(2,1)}) %all-gather.8.cloned.1.call-update) | async-done | bytes 1572880 | tf_op jit(solution)/shard_map/all_gather | solution.py:60
  86.4 71.1 %all-gather.10.cloned.1.call-done = bf16[1,1,48,128,128]{4,3,1,0,2:T(8,128)(2,1)} async-done(((bf16[1,1,3,128,128]{4,3,1,0,2:T(8,128)(2,1)}), bf16[1,1,48,128,128]{4,3,1,0,2:T(8,128)(2,1)}) %all-gather.10.cloned.1.call-update) | async-done | bytes 1572880 | tf_op jit(solution)/shard_map/all_gather | solution.py:61
  157.5 3.3 convolution_bitcast_fusion
  160.8 9.9 %fusion.20 = bf16[192,14,256]{2,1,0:T(8,128)(2,1)S(1)} fusion(f32[192,48,256]{2,0,1:T(8,128)S(1)} %convolution_bitcast_fusion, f32[48]{0:T(128)S(1)} %convert_element_type.64, s32[48]{0:T(128)S(1)} %get-tuple-element.6), kind=kOutput, calls=%fused_computation.23 | convolution fusion | flops 397051200 | bytes 10813824 | tf_op jit(solution)/shard_map/tsn,sc->tcn/dot_general | solution.py:31
  171.0 1.4 convert_element_type.68
  172.5 1.0 copy.54
  173.6 13.2 %all_gather.18 = bf16[192,1792]{1,0:T(8,128)(2,1)S(1)} all-gather(bf16[48,1792]{1,0:T(8,128)(2,1)S(1)} %copy-done.3), channel_id=1, replica_groups=mesh['dp'=16,'row'=4,'col'=8] {'row'}, dimensions={0}, use_global_device_ids=true | all-gather | bytes 860160 | tf_op jit(solution)/shard_map/all_gather | solution.py:48
  186.7 25.9 %all-gather.6.cloned.1.call-done = bf16[4,192,1792]{2,1,0:T(8,128)(2,1)} async-done(((bf16[1,192,1792]{2,1,0:T(8,128)(2,1)}), bf16[4,192,1792]{2,1,0:T(8,128)(2,1)}) %all-gather.6.cloned.1.call-update) | async-done | bytes 2752528 | tf_op jit(solution)/shard_map/all_gather | solution.py:68
  212.6 2.5 reduce_sum.32
  215.1 59.4 %all-reduce.2.cloned.1.call-done = bf16[192,1792]{1,0:T(8,128)(2,1)} async-done(((bf16[192,1792]{1,0:T(8,128)(2,1)}), bf16[192,1792]{1,0:T(8,128)(2,1)}) %all-reduce.2.cloned.1.call-update) | async-done | bytes 688144 | tf_op jit(solution)/shard_map/psum | solution.py:69
  274.5 1.9 fusion.36
  276.9 3.1 gather_fusion.1
  280.0 6.3 %multiply_convert_fusion = bf16[48,128,256]{2,1,0:T(8,128)(2,1)} fusion(f32[48]{0:T(128)S(1)} %convert_element_type.64, bf16[48,192,256]{2,1,0:T(8,128)(2,1)} %gather_fusion.1, pred[48]{0:T(512)(128)(4,1)S(1)} %get-tuple-element.5, bf16[48,192,128]{2,1,0:T(8,128)(2,1)} %copy-done, pred[48]{0:T(512)(128)(4,1)S(1)} %get-tuple-element.20), kind=kOutput, calls=%fused_computation.4 | convolution fusion | flops 610664448 | bytes 10223904 | tf_op jit(solution)/shard_map/tsk,tsn->skn/dot_general | solution.py:95
  286.6 1.1 copy-done.1
  288.2 3.3 fusion.10
  291.5 4.9 %fusion.32 = bf16[8,192,128]{2,0,1:T(8,128)(2,1)S(1)} fusion(f32[192,48,128]{2,0,1:T(8,128)S(1)} %fusion.10, f32[48]{0:T(128)S(1)} %convert_element_type.64, s32[48]{0:T(128)S(1)} %get-tuple-element.21), kind=kOutput, calls=%fused_computation.34 | convolution fusion | flops 113443584 | bytes 5112192 | tf_op jit(solution)/shard_map/tsk,sr->trk/dot_general | solution.py:38
  296.4 0.8 copy.57
  297.3 67.6 %reduce-scatter.5.cloned.1.call-done = bf16[3,128,256]{2,1,0:T(8,128)(2,1)} async-done(((bf16[48,128,256]{2,1,0:T(8,128)(2,1)}), bf16[3,128,256]{2,1,0:T(8,128)(2,1)}) %reduce-scatter.5.cloned.1.call-update) | async-done | bytes 196624 | tf_op jit(solution)/shard_map/reduce_scatter | solution.py:98
  364.8 1.0 convert_element_type.76
  365.8 0.8 fusion.37
  366.6 37.9 %reduce-scatter.3.cloned.1.call-done = bf16[24,1024]{1,0:T(8,128)(2,1)} async-done(((bf16[192,1024]{1,0:T(8,128)(2,1)}), bf16[24,1024]{1,0:T(8,128)(2,1)}) %reduce-scatter.3.cloned.1.call-update) | async-done | bytes 49168 | tf_op jit(solution)/shard_map/reduce_scatter | solution.py:86
  (33 shorter events, 3.8 us)
Async XLA Ops:
  7.2 79.3 %all-gather.8.cloned.1.call-start = ((), (), s32[]{:S(2)}) async-start(), calls=%async_computation.6 | async-start | bytes 1671168 | tf_op jit(solution)/shard_map/all_gather | solution.py:60
  7.9 149.6 %all-gather.10.cloned.1.call-start = ((), (), s32[]{:S(2)}) async-start(), calls=%async_computation.7 | async-start | bytes 1671168 | tf_op jit(solution)/shard_map/all_gather | solution.py:61
  8.6 203.9 %all-gather.6.cloned.1.call-start = ((), (), s32[]{:S(2)}) async-start(), calls=%async_computation.3 | async-start | bytes 3440640 | tf_op jit(solution)/shard_map/all_gather | solution.py:68
  24.7 136.1 %copy-start = (bf16[48,192,128]{2,1,0:T(8,128)(2,1)}, bf16[48,192,128]{2,1,0:T(8,128)(2,1)S(1)}, u32[]{:S(2)}) copy-start(bf16[48,192,128]{2,1,0:T(8,128)(2,1)S(1)} %gather_fusion) | copy-start | bytes 7077892
  171.0 2.5 copy-start.3
  172.4 102.1 %all-reduce.2.cloned.1.call-start = ((), (), s32[]{:S(2)}) async-start(), calls=%async_computation.2 | async-start | bytes 1376256 | tf_op jit(solution)/shard_map/psum | solution.py:69
  173.5 191.3 %reduce-scatter.5.cloned.1.call-start = ((), (), s32[]{:S(2)}) async-start(), calls=%async_computation.5 | async-start | bytes 3342336 | tf_op jit(solution)/shard_map/reduce_scatter | solution.py:98
  286.3 1.4 copy-start.1
  286.3 1.9 copy-start.2
  286.3 118.1 %reduce-scatter.3.cloned.1.call-start = ((), (), s32[]{:S(2)}) async-start(), calls=%async_computation.4 | async-start | bytes 442368 | tf_op jit(solution)/shard_map/reduce_scatter | solution.py:86
Sparse Core Ops, SparseCore 0:
  10.0 76.3 all-gather.7
  88.5 68.9 all-gather.9
  172.5 40.0 all-gather.5
  214.8 59.6 all-reduce.1
  286.4 78.3 reduce-scatter.4
  368.1 36.3 reduce-scatter.2
